TPU v7x, 32 devices: a whole 2x2x4 slice. The times are simulated.
32 devices in a mesh: visit: 8 (over z, x), sky: 4 (over y, core).
Axes of the slice: x: 2, y: 2, z: 4, core: 2. Of those that a mesh axis runs over, the one named last changes fastest.
Arguments:
- warped: bfloat16 [16, 512, 2048], P('visit', 'sky'), may hold values from -11 to 21
- inv_var: bfloat16 [16, 512, 2048], P('visit', 'sky'), may hold values from 0.19921875 to 5
- intersection: int32 [8, 4, 4], P('visit', 'sky'), may hold values from 0 to 3, as said below
- col_start: int32 [8, 4], P('visit', 'sky'), may hold values from 0 to 1536, as said below
- row_interp: bfloat16 [8, 4, 512, 512], P('visit', 'sky'), may hold values from -0.22 to 1.4, as said below
- col_interp: bfloat16 [8, 4, 512, 512], P('visit', 'sky'), may hold values from -0.22 to 1.4, as said below
- cell_ids: int32 [8, 4, 4, 4], P('visit', 'sky'), may hold values from 0 to 15
- kernels: bfloat16 [8, 4, 16, 121], P('visit', 'sky'), may hold values from -0.59765625 to 0.59765625
- science: bfloat16 [8, 4, 512, 512], P('visit', 'sky'), may hold values from -8 to 8
- inv_sigma: bfloat16 [8, 4, 512, 512], P('visit', 'sky'), may hold values from 0.29882812 to 1
Outputs:
- coadd: float32 [512, 2048], P('sky')
- outlier_weight: float32 [8, 4, 512, 512], P('visit', 'sky')
Inputs may be any that keep to these rules, and one draw needn't show every extreme that they name: `intersection`: the 4 strip numbers of one tile are distinct. `col_start`: a multiple of 128. `row_interp`: nonzero only within two places of the diagonal, each row's diagonal entry larger than the sum of its other magnitudes. `col_interp`: nonzero only within two places of the diagonal, each row's diagonal entry larger than the sum of its other magnitudes.
All inputs are finite; a program needn't handle non-finite values.
Results may differ from a plain program's by a relative error of at most 0.0017.
Values may be sent and summed in bfloat16 or wider, within the bound.
No kernel may reach another device: no remote copies, remote signals or barrier semaphores. Data moves between devices by JAX's collectives and lax.ppermute only.
A program may use at most 64 MiB of HBM per device.

v0:
```python
import jax
import jax.numpy as jnp
from jax import lax
from jax.sharding import PartitionSpec as P

STRIP = 128
NOV = 4
TILE = 512
KSIZE = 11
CELL = 128
NCELL = 16
PASSES = 3
CAUCHY = 2.0
OUTLIER = 3.0


def local_coadd(values, weights):
    root_weight = jnp.sqrt(weights)
    coadd_field = jnp.sum(weights * values, axis=0) / jnp.sum(weights, axis=0)
    for pass_index in range(PASSES):
        scaled = (values - coadd_field[None]) * root_weight / CAUCHY
        cauchy = weights / (1.0 + scaled * scaled)
        coadd_field = jnp.sum(cauchy * values, axis=0) / jnp.sum(cauchy, axis=0)
    return coadd_field


def psf_match(blotted, cell_grid, kernel_table):
    tile_side = blotted.shape[1]
    blocks = tile_side // CELL
    half_width = KSIZE // 2
    window = CELL + KSIZE - 1
    picker = (cell_grid.reshape(-1)[:, None] == jnp.arange(NCELL, dtype=jnp.int32)[None, :]).astype(
        jnp.bfloat16
    )
    tap_rows = jnp.dot(picker, kernel_table, preferred_element_type=jnp.float32)
    tap_rows = tap_rows.astype(jnp.bfloat16).reshape(blocks * blocks, KSIZE, KSIZE)
    source = jnp.arange(window, dtype=jnp.int32)[:, None]
    target = jnp.arange(CELL, dtype=jnp.int32)[None, :]
    diagonal = (
        (source - target)[None] == jnp.arange(KSIZE, dtype=jnp.int32)[:, None, None]
    ).astype(jnp.bfloat16)
    banded_all = jnp.einsum(
        "kab,bcl->kcal", tap_rows, diagonal, preferred_element_type=jnp.float32
    ).astype(jnp.bfloat16)
    banded_all = banded_all.reshape(blocks * blocks, window, KSIZE * CELL)
    padded = jnp.pad(blotted, ((half_width, half_width), (half_width, half_width)))
    row_parts = []
    for row_block in range(blocks):
        rows_window = lax.slice_in_dim(padded, row_block * CELL, row_block * CELL + window, axis=0)
        col_parts = []
        for col_block in range(blocks):
            cols_window = lax.slice_in_dim(
                rows_window, col_block * CELL, col_block * CELL + window, axis=1
            )
            horizontal = jnp.dot(
                cols_window,
                banded_all[row_block * blocks + col_block],
                preferred_element_type=jnp.float32,
            ).reshape(window, KSIZE, CELL)
            summed = horizontal[0:CELL, 0, :]
            for tap_row in range(1, KSIZE):
                summed = summed + horizontal[tap_row : tap_row + CELL, tap_row, :]
            col_parts.append(summed)
        row_parts.append(jnp.concatenate(col_parts, axis=1))
    return jnp.concatenate(row_parts, axis=0)


def shards(
    warped,
    inv_var,
    intersection,
    col_start,
    row_interp,
    col_interp,
    cell_ids,
    kernels,
    science,
    inv_sigma,
):
    n_visit = lax.axis_size("visit")
    n_sky = lax.axis_size("sky")
    local_visits, strip_rows, sky_w = warped.shape
    stacked = jnp.stack([warped, inv_var], axis=0)
    chunk = strip_rows // n_visit
    stacked = stacked.reshape(2, local_visits, n_visit, chunk, sky_w).transpose(2, 0, 1, 3, 4)
    stacked = stacked.reshape(n_visit, 2 * local_visits * chunk, sky_w)
    gathered = lax.all_to_all(stacked, "visit", split_axis=0, concat_axis=0, tiled=True)
    gathered = gathered.reshape(n_visit, 2, local_visits, chunk, sky_w)
    gathered = gathered.transpose(1, 0, 2, 3, 4).reshape(2, n_visit * local_visits, chunk, sky_w)
    row_share = local_coadd(gathered[0].astype(jnp.float32), gathered[1].astype(jnp.float32))
    copies = jnp.broadcast_to(row_share[None], (n_visit,) + row_share.shape)
    coadd_field = lax.all_to_all(copies, "visit", split_axis=0, concat_axis=0, tiled=True)
    coadd_field = coadd_field.reshape(n_visit * chunk, sky_w)
    coadd_low = coadd_field.astype(jnp.bfloat16)
    start_col = col_start[0, 0]
    all_starts = lax.all_gather(col_start[0], "sky", axis=0, tiled=True)
    windows = jnp.stack(
        [lax.dynamic_slice_in_dim(coadd_low, all_starts[peer], TILE, 1) for peer in range(n_sky)],
        axis=0,
    )
    strips_here = lax.all_to_all(windows, "sky", split_axis=0, concat_axis=0, tiled=True)
    strips = intersection[0, 0]
    footprint = jnp.concatenate(
        [
            lax.dynamic_index_in_dim(strips_here, strips[slot], 0, keepdims=False)
            for slot in range(NOV)
        ],
        axis=0,
    )
    projected = jnp.dot(row_interp[0, 0], footprint, preferred_element_type=jnp.float32).astype(
        jnp.bfloat16
    )
    blotted = jnp.dot(projected, col_interp[0, 0], preferred_element_type=jnp.float32).astype(
        jnp.bfloat16
    )
    matched = psf_match(blotted, cell_ids[0, 0], kernels[0, 0])
    residual = (
        (science[0, 0].astype(jnp.float32) - matched)
        * inv_sigma[0, 0].astype(jnp.float32)
        / OUTLIER
    )
    outlier = 1.0 / (1.0 + residual * residual)
    return (coadd_field, outlier[None, None])


def solution(mesh):
    in_specs = (
        P("visit", "sky", None),
        P("visit", "sky", None),
        P("visit", "sky", None),
        P("visit", "sky"),
        P("visit", "sky", None, None),
        P("visit", "sky", None, None),
        P("visit", "sky", None, None),
        P("visit", "sky", None, None),
        P("visit", "sky", None, None),
        P("visit", "sky", None, None),
    )
    out_specs = (P("sky", None), P("visit", "sky", None, None))
    return jax.shard_map(shards, mesh=mesh, in_specs=in_specs, out_specs=out_specs, check_vma=False)
```

profile of v0, /device:TPU:0, one launch (start us, length us, event | category | flops | bytes accessed | tf_op | source)
XLA Modules:
  0.0 227.3 jit_solution(4613131695956559904)
XLA Ops:
  0.6 1.8 maximum_bitcast_fusion
  2.7 55.3 %all_to_all.15 = bf16[8,64,2048]{2,1,0:T(8,128)(2,1)S(1)} all-to-all(bf16[8,64,2048]{2,1,0:T(8,128)(2,1)S(1)} %bitcast.262), channel_id=1, replica_groups=mesh['visit'=8,'sky'=4] {'visit'}, dimensions={0} | all-to-all | bytes 4194304 | tf_op jit(solution)/shard_map/all_to_all | solution.py:87
  58.4 1.3 fusion.23
  59.8 1.3 fusion.24
  61.1 1.3 fusion.25
  63.6 3.6 %all-to-all-start.1 = ((f32[8,16,2048]{2,1,0:T(8,128)}), f32[8,16,2048]{2,1,0:T(8,128)S(1)}, u32[]{:S(2)}, u32[]{:S(2)}) async-start(f32[8,16,2048]{2,1,0:T(8,128)} %broadcast_in_dim.2), calls=%async_computation.1 | async-start | bytes 2097152 | tf_op jit(solution)/shard_map/all_to_all | solution.py:92
  69.1 5.0 %all-reduce.1 = s32[4]{0:T(128)S(1)} all-reduce(s32[4]{0:T(128)S(1)} %bitcast_dynamic-update-slice_fusion), channel_id=2, replica_groups=mesh['visit'=8,'sky'=4] {'sky'}, use_global_device_ids=true, to_apply=%add.1 | all-reduce | flops 4 | bytes 32
  82.8 4.4 %convert_bitcast_fusion = bf16[16,138,11,128]{3,0,2,1:T(8,128)(2,1)} fusion(s32[138,128]{1,0:T(8,128)S(1)} %iota_subtract_fusion, bf16[16,11,11]{2,1,0:T(8,128)(2,1)S(1)} %reshape.203), kind=kOutput, calls=%fused_computation | convolution fusion | flops 71698176 | bytes 6292256 | tf_op jit(solution)/shard_map/kab,bcl->kcal/dot_general | solution.py:42
  87.2 5.6 %all-to-all-done.1 = f32[8,16,2048]{2,1,0:T(8,128)S(1)} async-done(((f32[8,16,2048]{2,1,0:T(8,128)}), f32[8,16,2048]{2,1,0:T(8,128)S(1)}, u32[]{:S(2)}, u32[]{:S(2)}) %all-to-all-start.1) | async-done | bytes 1048608 | tf_op jit(solution)/shard_map/all_to_all | solution.py:92
  94.0 4.3 %all-to-all-start.2 = ((bf16[4,128,512]{2,1,0:T(8,128)(2,1)}), bf16[4,128,512]{2,1,0:T(8,128)(2,1)}, u32[]{:S(2)}, u32[]{:S(2)}) async-start(bf16[4,128,512]{2,1,0:T(8,128)(2,1)} %pad_maximum_fusion), calls=%async_computation.2 | async-start | bytes 1048576 | tf_op jit(solution)/shard_map/all_to_all | solution.py:101
  98.4 46.7 %slice_reduce_fusion.15 = (bf16[138,11,128]{2,1,0:T(8,128)(2,1)}, bf16[138,11,128]{2,1,0:T(8,128)(2,1)}, bf16[138,11,128]{2,1,0:T(8,128)(2,1)}, bf16[138,11,128]...) fusion(bf16[16,138,11,128]{3,0,2,1:T(8,128)(2,1)} %convert_bitc, ...), kind=kLoop, calls=%fused_computation.56 | loop fusion | bytes 12435456 | tf_op jit(solution)/shard_map/slice | solution.py:57
  150.4 1.2 pad.35
  152.5 2.1 dot_general.129
  154.5 1.2 pad.50
  156.6 2.1 dot_general.174
  158.6 1.2 pad.49
  160.7 2.1 dot_general.171
  162.8 1.2 pad.48
  164.8 2.1 dot_general.168
  168.9 2.1 dot_general.165
  173.0 2.1 dot_general.162
  177.1 2.1 dot_general.159
  181.2 2.1 dot_general.156
  185.3 2.1 dot_general.153
  189.4 2.1 dot_general.150
  193.6 2.1 dot_general.147
  197.7 2.1 dot_general.144
  201.8 2.1 dot_general.141
  204.9 1.3 dot_general.138
  211.2 1.8 dynamic-slice_bitcast_fusion.3
  213.0 2.1 convolution_convert_fusion
  225.0 1.3 fusion.22
  (129 shorter events, 41.8 us)
Async XLA Ops:
  0.6 212.4 %copy-start = (bf16[1,1,512,512]{3,2,1,0:T(8,128)(2,1)S(1)}, bf16[1,1,512,512]{3,2,1,0:T(8,128)(2,1)}, u32[]{:S(2)}) copy-start(bf16[1,1,512,512]{3,2,1,0:T(8,128)(2,1)} %param.15) | copy-start | bytes 1572868
  62.4 5.4 %copy-start.21 = (u32[32]{0:T(128)S(1)}, u32[32]{0:T(128)}, u32[]{:S(2)}) copy-start(u32[32]{0:T(128)} %constant.44) | copy-start | bytes 388
  62.5 17.4 %copy-start.19 = (s32[1,1,4,4]{3,2,1,0:T(4,128)S(1)}, s32[1,1,4,4]{3,2,1,0:T(4,128)}, u32[]{:S(2)}) copy-start(s32[1,1,4,4]{3,2,1,0:T(4,128)} %param.16) | copy-start | bytes 196
  62.5 17.4 %copy-start.20 = (bf16[1,1,16,121]{3,2,1,0:T(8,128)(2,1)S(1)}, bf16[1,1,16,121]{3,2,1,0:T(8,128)(2,1)}, u32[]{:S(2)}) copy-start(bf16[1,1,16,121]{3,2,1,0:T(8,128)(2,1)} %param.17) | copy-start | bytes 11620
  63.6 29.2 %all-to-all-start.1 = ((f32[8,16,2048]{2,1,0:T(8,128)}), f32[8,16,2048]{2,1,0:T(8,128)S(1)}, u32[]{:S(2)}, u32[]{:S(2)}) async-start(f32[8,16,2048]{2,1,0:T(8,128)} %broadcast_in_dim.2), calls=%async_computation.1 | async-start | bytes 2097152 | tf_op jit(solution)/shard_map/all_to_all | solution.py:92
  94.0 117.1 %all-to-all-start.2 = ((bf16[4,128,512]{2,1,0:T(8,128)(2,1)}), bf16[4,128,512]{2,1,0:T(8,128)(2,1)}, u32[]{:S(2)}, u32[]{:S(2)}) async-start(bf16[4,128,512]{2,1,0:T(8,128)(2,1)} %pad_maximum_fusion), calls=%async_computation.2 | async-start | bytes 1048576 | tf_op jit(solution)/shard_map/all_to_all | solution.py:101
  98.4 46.7 %copy-start.18 = (s32[1,1,4]{2,1,0:T(1,128)S(1)}, s32[1,1,4]{2,1,0:T(1,128)}, u32[]{:S(2)}) copy-start(s32[1,1,4]{2,1,0:T(1,128)} %param.12) | copy-start | bytes 52
  213.0 2.1 copy-start.1
  215.1 1.1 copy-start.2
  215.1 1.4 copy-start.3
  216.2 1.1 copy-start.4
  216.6 1.1 copy-start.5
  217.3 1.1 copy-start.6
  217.7 1.1 copy-start.7
  218.4 1.1 copy-start.8
  219.0 1.1 copy-start.9
  219.5 1.1 copy-start.10
  220.1 1.1 copy-start.11
  220.6 1.1 copy-start.12
  221.2 1.1 copy-start.13
  222.3 1.1 copy-start.15
  222.7 1.1 copy-start.14
  223.8 1.0 copy-start.16
  223.8 1.2 copy-start.17
where the time goes:
time: 229 us; the launch traced here: 227 us
  local copies, waits for them, and re-layouts  115 us (50%)
  blocking collectives  60.3 us (26%)
  between operations  16.8 us (7%)
  matrix products  11.7 us (5%)
  other arithmetic  9.64 us (4%)
  starting transfers between devices  7.91 us (3%)
  waiting for transfers between devices  5.6 us (2%)
    all_to_all x1, blocking collectives, shards(): lax.all_to_all(stacked, 'visit', split_axis=0, concat_axis=0, tiled=True)  55.3 us
    slice x1, local copies, waits for them, and re-layouts, psf_match(): banded_all[row_block * blocks + col_block]  46.7 us
    unnamed x80, local copies, waits for them, and re-layouts  33.4 us
    dot_general x16, local copies, waits for them, and re-layouts, psf_match(): jnp.dot(cols_window, banded_all[row_block * blocks + col_block], preferre...  30.4 us
    all_to_all x1, waiting for transfers between devices, shards(): lax.all_to_all(copies, 'visit', split_axis=0, concat_axis=0, tiled=True)  5.6 us
    dot_general x16, matrix products, psf_match(): jnp.dot(cols_window, banded_all[row_block * blocks + col_block], preferre...  5.03 us
    unnamed x1, blocking collectives  4.97 us
  transfers between devices with their start and end apart: 2, of which 1 were waited for; matrix products, arithmetic and copies ran while one was open for 49% of the time, Pallas kernels for 0%

commit v1 on v0

--- a/solution.py
+++ b/solution.py
@@ -12,6 +12,17 @@
 PASSES = 3
 CAUCHY = 2.0
 OUTLIER = 3.0
+
+
+def cut_along(x, dim, size):
+    before, after = (x.shape[:dim], x.shape[dim + 1 :])
+    return jnp.moveaxis(x.reshape(*before, size, -1, *after), dim, 0)
+
+
+def joined_along(blocks, dim):
+    blocks = jnp.moveaxis(blocks, 0, dim)
+    shape = blocks.shape
+    return blocks.reshape(*shape[:dim], shape[dim] * shape[dim + 1], *shape[dim + 2 :])
 
 
 def local_coadd(values, weights):
@@ -84,7 +95,14 @@
     chunk = strip_rows // n_visit
     stacked = stacked.reshape(2, local_visits, n_visit, chunk, sky_w).transpose(2, 0, 1, 3, 4)
     stacked = stacked.reshape(n_visit, 2 * local_visits * chunk, sky_w)
-    gathered = lax.all_to_all(stacked, "visit", split_axis=0, concat_axis=0, tiled=True)
+    peers, mine = (lax.axis_size("visit"), lax.axis_index("visit"))
+    blocks_2 = cut_along(stacked, 0, peers)
+    done = [blocks_2[mine]]
+    for lap in range(1, peers):
+        sent = blocks_2[mine ^ lap]
+        done.append(lax.ppermute(sent, "visit", [(i, i ^ lap) for i in range(peers)]))
+    blocks_2 = jnp.stack(done)[mine ^ jnp.arange(peers)]
+    gathered = joined_along(blocks_2, 0)
     gathered = gathered.reshape(n_visit, 2, local_visits, chunk, sky_w)
     gathered = gathered.transpose(1, 0, 2, 3, 4).reshape(2, n_visit * local_visits, chunk, sky_w)
     row_share = local_coadd(gathered[0].astype(jnp.float32), gathered[1].astype(jnp.float32))

time: 229 us -> 236 us (1.031)
  blocking collectives: 60.3 us -> 4.97 us
  waiting for transfers between devices: 5.6 us -> 43.2 us
  starting transfers between devices: 7.91 us -> 21.2 us
  local copies, waits for them, and re-layouts: 115 us -> 126 us
    all_to_all x1 -> x0, blocking collectives: 55.3 us -> none  [shards(): lax.all_to_all(stacked, 'visit', split_axis=0, concat_axis=0, tiled=True)]
    ppermute x0 -> x7, waiting for transfers between devices: none -> 38.7 us  [shards(): lax.ppermute(sent, 'visit', [(i, i ^ lap) for i in range(peers)])]
    ppermute x0 -> x7, starting transfers between devices: none -> 14 us  [shards(): lax.ppermute(sent, 'visit', [(i, i ^ lap) for i in range(peers)])]
    unnamed x80 -> x88, local copies, waits for them, and re-layouts: 33.4 us -> 40.2 us
  transfers between devices with their start and end apart: 2 -> 9, of which waited for: 1 -> 4; matrix products, arithmetic and copies ran while one was open for 49% -> 51% of each run, Pallas kernels for 0% -> 0%
where the time goes in v1:
time: 236 us; the launch traced here: 234 us
  local copies, waits for them, and re-layouts  126 us (53%)
  waiting for transfers between devices  43.2 us (18%)
  starting transfers between devices  21.2 us (9%)
  between operations  16.5 us (7%)
  matrix products  11.7 us (5%)
  other arithmetic  9.92 us (4%)
  blocking collectives  4.97 us (2%)
    slice x1, local copies, waits for them, and re-layouts, psf_match(): banded_all[row_block * blocks + col_block]  46.8 us
    unnamed x88, local copies, waits for them, and re-layouts  40.2 us
    ppermute x7, waiting for transfers between devices, shards(): lax.ppermute(sent, 'visit', [(i, i ^ lap) for i in range(peers)])  38.7 us
    dot_general x16, local copies, waits for them, and re-layouts, psf_match(): jnp.dot(cols_window, banded_all[row_block * blocks + col_block], preferre...  31.4 us
    ppermute x7, starting transfers between devices, shards(): lax.ppermute(sent, 'visit', [(i, i ^ lap) for i in range(peers)])  14 us
    dot_general x16, matrix products, psf_match(): jnp.dot(cols_window, banded_all[row_block * blocks + col_block], preferre...  5.05 us
    unnamed x1, blocking collectives  4.97 us
  transfers between devices with their start and end apart: 9, of which 4 were waited for; matrix products, arithmetic and copies ran while one was open for 51% of the time, Pallas kernels for 0%

profile of v1, /device:TPU:0, one launch (start us, length us, event | category | flops | bytes accessed | tf_op | source)
XLA Modules:
  0.0 233.7 jit_solution(7272458129251025500)
XLA Ops:
  0.7 1.8 maximum_bitcast_fusion
  3.6 3.0 %collective-permute-start = (bf16[1,64,2048]{2,1,0:T(8,128)(2,1)S(1)}, bf16[1,64,2048]{2,1,0:T(8,128)(2,1)S(1)}, u32[]{:S(2)}, u32[]{:S(2)}) collective-permute-start(bf16[1,64,2048]{2,1,0:T(8,128)(2,1)S(1)} %get-tuple-element.32), channel_id=1, source_target_pairs={{0,4},{4,0},{8,12},{12,8},{16,20},{20,16},{24,28},{28,24},{1,5},{5... | collective-permute-start | bytes 786440 | tf_op jit(solution)/shard_map/ppermute | solution.py:103
  6.6 3.6 %collective-permute-start.6 = (bf16[1,64,2048]{2,1,0:T(8,128)(2,1)S(1)}, bf16[1,64,2048]{2,1,0:T(8,128)(2,1)S(1)}, u32[]{:S(2)}, u32[]{:S(2)}) collective-permute-start(bf16[1,64,2048]{2,1,0:T(8,128)(2,1)S(1)} %get-tuple-element.26), channel_id=1, source_target_pairs={{0,28},{4,24},{8,20},{12,16},{16,12},{20,8},{24,4},{28,0},{1,29},{... | collective-permute-start | bytes 786440 | tf_op jit(solution)/shard_map/ppermute | solution.py:103
  10.2 1.9 collective-permute-start.4
  12.1 2.1 collective-permute-start.3
  14.2 4.2 %collective-permute-done = bf16[1,64,2048]{2,1,0:T(8,128)(2,1)S(1)} collective-permute-done((bf16[1,64,2048]{2,1,0:T(8,128)(2,1)S(1)}, bf16[1,64,2048]{2,1,0:T(8,128)(2,1)S(1)}, u32[]{:S(2)}, u32[]{:S(2)}) %collective-permute-start) | collective-permute-done | bytes 262176 | tf_op jit(solution)/shard_map/ppermute | solution.py:103
  19.2 18.8 %collective-permute-done.1 = bf16[1,64,2048]{2,1,0:T(8,128)(2,1)S(1)} collective-permute-done((bf16[1,64,2048]{2,1,0:T(8,128)(2,1)S(1)}, bf16[1,64,2048]{2,1,0:T(8,128)(2,1)S(1)}, u32[]{:S(2)}, u32[]{:S(2)}) %collective-permute-start.1) | collective-permute-done | bytes 262176 | tf_op jit(solution)/shard_map/ppermute | solution.py:103
  37.9 3.4 %collective-permute-start.2 = (bf16[1,64,2048]{2,1,0:T(8,128)(2,1)S(1)}, bf16[1,64,2048]{2,1,0:T(8,128)(2,1)S(1)}, u32[]{:S(2)}, u32[]{:S(2)}) collective-permute-start(bf16[1,64,2048]{2,1,0:T(8,128)(2,1)S(1)} %get-tuple-element.30), channel_id=1, source_target_pairs={{0,12},{4,8},{8,4},{12,0},{16,28},{20,24},{24,20},{28,16},{1,13},{... | collective-permute-start | bytes 786440 | tf_op jit(solution)/shard_map/ppermute | solution.py:103
  42.1 15.7 %collective-permute-done.2 = bf16[1,64,2048]{2,1,0:T(8,128)(2,1)S(1)} collective-permute-done((bf16[1,64,2048]{2,1,0:T(8,128)(2,1)S(1)}, bf16[1,64,2048]{2,1,0:T(8,128)(2,1)S(1)}, u32[]{:S(2)}, u32[]{:S(2)}) %collective-permute-start.2) | collective-permute-done | bytes 262176 | tf_op jit(solution)/shard_map/ppermute | solution.py:103
  61.5 2.3 gather_fusion
  64.2 1.3 fusion.23
  69.3 3.6 %all-to-all-start = ((f32[8,16,2048]{2,1,0:T(8,128)}), f32[8,16,2048]{2,1,0:T(8,128)S(1)}, u32[]{:S(2)}, u32[]{:S(2)}) async-start(f32[8,16,2048]{2,1,0:T(8,128)} %broadcast_in_dim.2), calls=%async_computation | async-start | bytes 2097152 | tf_op jit(solution)/shard_map/all_to_all | solution.py:110
  74.8 5.0 %all-reduce.1 = s32[4]{0:T(128)S(1)} all-reduce(s32[4]{0:T(128)S(1)} %bitcast_dynamic-update-slice_fusion.7), channel_id=2, replica_groups=mesh['visit'=8,'sky'=4] {'sky'}, use_global_device_ids=true, to_apply=%add.1 | all-reduce | flops 4 | bytes 32
  88.5 4.4 %convert_bitcast_fusion = bf16[16,138,11,128]{3,0,2,1:T(8,128)(2,1)} fusion(s32[138,128]{1,0:T(8,128)S(1)} %iota_subtract_fusion, bf16[16,11,11]{2,1,0:T(8,128)(2,1)S(1)} %reshape.211), kind=kOutput, calls=%fused_computation.1 | convolution fusion | flops 71698176 | bytes 6292256 | tf_op jit(solution)/shard_map/kab,bcl->kcal/dot_general | solution.py:53
  92.9 4.5 %all-to-all-done = f32[8,16,2048]{2,1,0:T(8,128)S(1)} async-done(((f32[8,16,2048]{2,1,0:T(8,128)}), f32[8,16,2048]{2,1,0:T(8,128)S(1)}, u32[]{:S(2)}, u32[]{:S(2)}) %all-to-all-start) | async-done | bytes 1048608 | tf_op jit(solution)/shard_map/all_to_all | solution.py:110
  98.7 3.6 %all-to-all-start.1 = ((bf16[4,128,512]{2,1,0:T(8,128)(2,1)}), bf16[4,128,512]{2,1,0:T(8,128)(2,1)S(1)}, u32[]{:S(2)}, u32[]{:S(2)}) async-start(bf16[4,128,512]{2,1,0:T(8,128)(2,1)} %pad_maximum_fusion), calls=%async_computation.1 | async-start | bytes 1048576 | tf_op jit(solution)/shard_map/all_to_all | solution.py:119
  102.3 46.8 %slice_reduce_fusion.15 = (bf16[138,11,128]{2,1,0:T(8,128)(2,1)}, bf16[138,11,128]{2,1,0:T(8,128)(2,1)}, bf16[138,11,128]{2,1,0:T(8,128)(2,1)}, bf16[138,11,128]...) fusion(bf16[16,138,11,128]{3,0,2,1:T(8,128)(2,1)} %convert_bitc, ...), kind=kLoop, calls=%fused_computation.57 | loop fusion | bytes 12435456 | tf_op jit(solution)/shard_map/slice | solution.py:68
  156.5 2.1 dot_general.129
  160.6 2.1 dot_general.174
  164.7 2.1 dot_general.171
  168.8 2.1 dot_general.168
  172.9 2.1 dot_general.165
  177.0 2.1 dot_general.162
  181.1 2.1 dot_general.159
  185.3 2.1 dot_general.156
  189.4 2.1 dot_general.153
  193.5 2.1 dot_general.150
  197.6 2.1 dot_general.147
  201.7 2.1 dot_general.144
  205.8 2.1 dot_general.141
  210.0 2.1 dot_general.138
  219.5 2.1 convolution_convert_fusion
  (155 shorter events, 60.1 us)
Async XLA Ops:
  0.6 218.8 %copy-start = (bf16[1,1,512,512]{3,2,1,0:T(8,128)(2,1)S(1)}, bf16[1,1,512,512]{3,2,1,0:T(8,128)(2,1)}, u32[]{:S(2)}) copy-start(bf16[1,1,512,512]{3,2,1,0:T(8,128)(2,1)} %param.15) | copy-start | bytes 1572868
  3.6 14.9 %collective-permute-start = (bf16[1,64,2048]{2,1,0:T(8,128)(2,1)S(1)}, bf16[1,64,2048]{2,1,0:T(8,128)(2,1)S(1)}, u32[]{:S(2)}, u32[]{:S(2)}) collective-permute-start(bf16[1,64,2048]{2,1,0:T(8,128)(2,1)S(1)} %get-tuple-element.32), channel_id=1, source_target_pairs={{0,4},{4,0},{8,12},{12,8},{16,20},{20,16},{24,28},{28,24},{1,5},{5... | collective-permute-start | bytes 786440 | tf_op jit(solution)/shard_map/ppermute | solution.py:103
  6.6 54.2 %collective-permute-start.6 = (bf16[1,64,2048]{2,1,0:T(8,128)(2,1)S(1)}, bf16[1,64,2048]{2,1,0:T(8,128)(2,1)S(1)}, u32[]{:S(2)}, u32[]{:S(2)}) collective-permute-start(bf16[1,64,2048]{2,1,0:T(8,128)(2,1)S(1)} %get-tuple-element.26), channel_id=1, source_target_pairs={{0,28},{4,24},{8,20},{12,16},{16,12},{20,8},{24,4},{28,0},{1,29},{... | collective-permute-start | bytes 786440 | tf_op jit(solution)/shard_map/ppermute | solution.py:103
  10.1 49.9 %collective-permute-start.5 = (bf16[1,64,2048]{2,1,0:T(8,128)(2,1)S(1)}, bf16[1,64,2048]{2,1,0:T(8,128)(2,1)S(1)}, u32[]{:S(2)}, u32[]{:S(2)}) collective-permute-start(bf16[1,64,2048]{2,1,0:T(8,128)(2,1)S(1)} %get-tuple-element.27), channel_id=1, source_target_pairs={{0,24},{4,28},{8,16},{12,20},{16,8},{20,12},{24,0},{28,4},{1,25},{... | collective-permute-start | bytes 786440 | tf_op jit(solution)/shard_map/ppermute | solution.py:103
  10.2 49.1 %collective-permute-start.4 = (bf16[1,64,2048]{2,1,0:T(8,128)(2,1)S(1)}, bf16[1,64,2048]{2,1,0:T(8,128)(2,1)S(1)}, u32[]{:S(2)}, u32[]{:S(2)}) collective-permute-start(bf16[1,64,2048]{2,1,0:T(8,128)(2,1)S(1)} %get-tuple-element.28), channel_id=1, source_target_pairs={{0,20},{4,16},{8,28},{12,24},{16,4},{20,0},{24,12},{28,8},{1,21},{... | collective-permute-start | bytes 786440 | tf_op jit(solution)/shard_map/ppermute | solution.py:103
  12.1 46.4 %collective-permute-start.3 = (bf16[1,64,2048]{2,1,0:T(8,128)(2,1)S(1)}, bf16[1,64,2048]{2,1,0:T(8,128)(2,1)S(1)}, u32[]{:S(2)}, u32[]{:S(2)}) collective-permute-start(bf16[1,64,2048]{2,1,0:T(8,128)(2,1)S(1)} %get-tuple-element.29), channel_id=1, source_target_pairs={{0,16},{4,20},{8,24},{12,28},{16,0},{20,4},{24,8},{28,12},{1,17},{... | collective-permute-start | bytes 786440 | tf_op jit(solution)/shard_map/ppermute | solution.py:103
  18.5 19.5 %collective-permute-start.1 = (bf16[1,64,2048]{2,1,0:T(8,128)(2,1)S(1)}, bf16[1,64,2048]{2,1,0:T(8,128)(2,1)S(1)}, u32[]{:S(2)}, u32[]{:S(2)}) collective-permute-start(bf16[1,64,2048]{2,1,0:T(8,128)(2,1)S(1)} %get-tuple-element.31), channel_id=1, source_target_pairs={{0,8},{4,12},{8,0},{12,4},{16,24},{20,28},{24,16},{28,20},{1,9},{5... | collective-permute-start | bytes 786440 | tf_op jit(solution)/shard_map/ppermute | solution.py:103
  37.9 19.9 %collective-permute-start.2 = (bf16[1,64,2048]{2,1,0:T(8,128)(2,1)S(1)}, bf16[1,64,2048]{2,1,0:T(8,128)(2,1)S(1)}, u32[]{:S(2)}, u32[]{:S(2)}) collective-permute-start(bf16[1,64,2048]{2,1,0:T(8,128)(2,1)S(1)} %get-tuple-element.30), channel_id=1, source_target_pairs={{0,12},{4,8},{8,4},{12,0},{16,28},{20,24},{24,20},{28,16},{1,13},{... | collective-permute-start | bytes 786440 | tf_op jit(solution)/shard_map/ppermute | solution.py:103
  68.2 5.4 %copy-start.22 = (u32[32]{0:T(128)S(1)}, u32[32]{0:T(128)}, u32[]{:S(2)}) copy-start(u32[32]{0:T(128)} %constant.67) | copy-start | bytes 388
  68.2 17.3 %copy-start.20 = (s32[1,1,4,4]{3,2,1,0:T(4,128)S(1)}, s32[1,1,4,4]{3,2,1,0:T(4,128)}, u32[]{:S(2)}) copy-start(s32[1,1,4,4]{3,2,1,0:T(4,128)} %param.16) | copy-start | bytes 196
  68.2 17.4 %copy-start.21 = (bf16[1,1,16,121]{3,2,1,0:T(8,128)(2,1)S(1)}, bf16[1,1,16,121]{3,2,1,0:T(8,128)(2,1)}, u32[]{:S(2)}) copy-start(bf16[1,1,16,121]{3,2,1,0:T(8,128)(2,1)} %param.17) | copy-start | bytes 11620
  69.3 28.1 %all-to-all-start = ((f32[8,16,2048]{2,1,0:T(8,128)}), f32[8,16,2048]{2,1,0:T(8,128)S(1)}, u32[]{:S(2)}, u32[]{:S(2)}) async-start(f32[8,16,2048]{2,1,0:T(8,128)} %broadcast_in_dim.2), calls=%async_computation | async-start | bytes 2097152 | tf_op jit(solution)/shard_map/all_to_all | solution.py:110
  98.7 120.0 %all-to-all-start.1 = ((bf16[4,128,512]{2,1,0:T(8,128)(2,1)}), bf16[4,128,512]{2,1,0:T(8,128)(2,1)S(1)}, u32[]{:S(2)}, u32[]{:S(2)}) async-start(bf16[4,128,512]{2,1,0:T(8,128)(2,1)} %pad_maximum_fusion), calls=%async_computation.1 | async-start | bytes 1048576 | tf_op jit(solution)/shard_map/all_to_all | solution.py:119
  102.3 46.9 %copy-start.19 = (s32[1,1,4]{2,1,0:T(1,128)S(1)}, s32[1,1,4]{2,1,0:T(1,128)}, u32[]{:S(2)}) copy-start(s32[1,1,4]{2,1,0:T(1,128)} %param.12) | copy-start | bytes 52
  213.2 2.1 copy-start.16
  219.5 2.1 copy-start.1
  221.6 1.1 copy-start.2
  221.6 1.4 copy-start.3
  222.6 1.1 copy-start.4
  223.0 1.1 copy-start.5
  223.7 1.1 copy-start.6
  224.1 1.3 copy-start.7
  224.8 1.1 copy-start.8
  225.5 1.1 copy-start.9
  225.9 1.1 copy-start.10
  226.6 1.1 copy-start.11
  227.0 1.1 copy-start.12
  227.7 1.1 copy-start.13
  228.1 1.1 copy-start.14
  228.8 1.1 copy-start.15
  230.3 1.0 copy-start.17
  230.3 1.2 copy-start.18
